TPU v7x, 32 devices: a whole 2x2x4 slice. The times are simulated.
32 devices in a mesh: ta: 8 (over z, y), col: 4 (over x, core).
Axes of the slice: x: 2, y: 2, z: 4, core: 2. Of those that a mesh axis runs over, the one named last changes fastest.
Arguments:
- strain: bfloat16 [2048, 512], P('col', 'ta'), may hold values from -6 to 6
- filter_taps: float32 [64], replicated, may hold values from -0.75 to 0.75
Outputs:
- cross_spectra: bfloat16 [4, 512, 128, 256], P('col', 'ta')
All inputs are finite; a program needn't handle non-finite values.
Results may differ from a plain program's by a relative error of at most 0.0066.
Values may be sent and summed in bfloat16 or wider, within the bound.
No kernel may reach another device: no remote copies, remote signals or barrier semaphores. Data moves between devices by JAX's collectives and lax.ppermute only.
A program may use at most 64 MiB of HBM per device.

v0:
```python
import jax
import jax.numpy as jnp
from jax import lax
from jax.sharding import PartitionSpec as P

NFFT = 256
NF = 128
LAGS = 128


def shifted(block, axis, distance):
    devices = range(lax.axis_size(axis))
    route = [((i - distance) % len(devices), i) for i in devices]
    return lax.ppermute(block, axis, route)


def from_behind(block, axis, distance):
    devices = range(lax.axis_size(axis))
    route = [(i - distance, i) for i in devices if i - distance in devices]
    return lax.ppermute(block, axis, route)


def tap_rows(filter_taps, outputs):
    tap_count = filter_taps.shape[0]
    window = 2 * outputs + tap_count
    flipped = filter_taps[::-1]
    period = jnp.concatenate([flipped, jnp.zeros((window + 2 - tap_count,), jnp.float32)])
    repeated = jnp.tile(period, outputs)[: outputs * window]
    return repeated.reshape(outputs, window)


def decimate(history, samples, filter_taps):
    channels, length = samples.shape
    tap_count = filter_taps.shape[0]
    outputs = min(length, NFFT) // 2
    blocks = length // (2 * outputs)
    joined = jnp.concatenate(
        [history, samples, jnp.zeros((channels, 2 * outputs - tap_count), jnp.float32)], axis=1
    )
    joined = joined.reshape(channels, blocks + 1, 2 * outputs)
    windows = jnp.concatenate([joined[:, :-1], joined[:, 1:, :tap_count]], axis=2)
    matrix = tap_rows(filter_taps, outputs)
    result = jnp.einsum("cbw,tw->cbt", windows, matrix, precision=lax.Precision.HIGHEST)
    return result.reshape(channels, blocks * outputs).astype(jnp.bfloat16)


def fourier_table():
    moment = lax.broadcasted_iota(jnp.int32, (NFFT, NF), 0)
    frequency = lax.broadcasted_iota(jnp.int32, (NFFT, NF), 1) + 1
    phase_index = moment * frequency % NFFT
    angles = phase_index.astype(jnp.float32) * (2.0 * jnp.pi / NFFT)
    window_taper = 0.5 - 0.5 * jnp.cos(moment.astype(jnp.float32) * (2.0 * jnp.pi / NFFT))
    return jnp.concatenate(
        [window_taper * jnp.cos(angles), -window_taper * jnp.sin(angles)], axis=1
    )


def whiten(filtered):
    channels, length = filtered.shape
    pieces = filtered.reshape(channels, length // NF, NF)
    segment_rows = jnp.concatenate([pieces[:, :-1], pieces[:, 1:]], axis=2)
    spectrum = jnp.einsum(
        "csn,nf->csf",
        segment_rows.astype(jnp.float32),
        fourier_table(),
        precision=lax.Precision.HIGHEST,
    )
    real_part = spectrum[..., :NF]
    imag_part = spectrum[..., NF:]
    powers = real_part * real_part + imag_part * imag_part
    mean_power = jnp.mean(powers, axis=-1, keepdims=True)
    whitening = 1.0 / jnp.sqrt(powers + mean_power + 1e-06)
    return jnp.concatenate([real_part * whitening, imag_part * whitening], axis=-1).astype(
        jnp.bfloat16
    )


def cross_block(own_rows, extended):
    rows, segments, columns = own_rows.shape
    own_pairs = own_rows.reshape(rows, 2 * segments, NF)
    turned = jnp.concatenate([-extended[..., NF:], extended[..., :NF]], axis=-1)
    far_pairs = jnp.stack(
        [extended.reshape(-1, 2 * segments, NF), turned.reshape(-1, 2 * segments, NF)], axis=2
    )
    step_rows = min(16, rows)
    reach = step_rows + LAGS
    results = []
    for first in range(0, rows, step_rows):
        own_part = own_pairs[first : first + step_rows]
        far_part = far_pairs[first : first + reach]
        combined = jnp.einsum(
            "cxf,dxof->cdof", own_part, far_part, preferred_element_type=jnp.float32
        )
        combined = combined.reshape(step_rows * reach, NFFT) / segments
        combined = jnp.concatenate([combined, jnp.zeros((step_rows, NFFT), jnp.float32)], axis=0)
        banded = combined.reshape(step_rows, reach + 1, NFFT)[:, :LAGS]
        results.append(banded.astype(jnp.bfloat16))
    return jnp.concatenate(results, axis=0)


def body(strain, filter_taps):
    tap_count = filter_taps.shape[0]
    regrouped = lax.all_to_all(strain, "ta", split_axis=0, concat_axis=1, tiled=True)
    filtered = decimate(
        jnp.zeros((regrouped.shape[0], tap_count), jnp.float32),
        regrouped.astype(jnp.float32),
        filter_taps,
    )
    whitened = whiten(filtered)
    block_rows, segments, columns = whitened.shape
    reach = LAGS // block_rows
    position = lax.axis_index("ta")
    extent = lax.axis_size("ta")
    pieces = []
    for offset in range(1, reach + 1):
        pieces.append(shifted(whitened, "ta", -offset))
    stacked = jnp.stack(pieces)
    beyond = from_behind(stacked, "col", -1)
    offsets_ahead = jnp.arange(1, reach + 1, dtype=jnp.int32).reshape(reach, 1, 1, 1)
    beyond_end = position + offsets_ahead >= extent
    chosen = jnp.where(beyond_end, beyond, stacked)
    ahead_rows = chosen.reshape(reach * block_rows, segments, columns)
    extended = jnp.concatenate([whitened, ahead_rows], axis=0)
    return cross_block(whitened, extended)[None]


def solution(mesh):
    return jax.shard_map(
        body,
        mesh=mesh,
        in_specs=(P("col", "ta"), P()),
        out_specs=P("col", "ta", None, None),
        check_vma=False,
    )
```

profile of v0, /device:TPU:1, one launch (start us, length us, event | category | flops | bytes accessed | tf_op | source)
XLA Modules:
  0.0 51.3 jit_solution(17561312377843437521)
XLA Ops:
  0.0 1.0 %copy.24 = bf16[512,64]{1,0:T(8,128)(2,1)S(1)} copy(bf16[512,64]{0,1:T(8,128)(2,1)} %param.2) | data formatting | bytes 131072 | tf_op args[0]
  1.0 0.8 %reshape.138 = bf16[8,2,2048]{2,1,0:T(2,128)(2,1)} reshape(bf16[8,64,64]{2,1,0:T(8,128)(2,1)S(1)} %bitcast.78) | data formatting | bytes 131072
  1.8 6.4 %all-to-all-start = ((bf16[8,2,2048]{2,1,0:T(2,128)(2,1)}), bf16[8,2,2048]{2,1,0:T(2,128)(2,1)S(1)}, u32[]{:S(2)}, u32[]{:S(2)}) async-start(bf16[8,2,2048]{2,1,0:T(2,128)(2,1)} %reshape.138), calls=%async_computation | async-start | bytes 131072 | tf_op jit(solution)/shard_map/all_to_all | solution.py:103
  8.7 0.7 %rev.3 = f32[64]{0:T(128)S(1)} reverse(f32[64]{0:T(128)} %param.3), dimensions={0} | reverse | bytes 512 | tf_op jit(solution)/shard_map/rev | solution.py:26
  10.0 3.9 %all-to-all-done = bf16[8,2,2048]{2,1,0:T(2,128)(2,1)S(1)} async-done(((bf16[8,2,2048]{2,1,0:T(2,128)(2,1)}), bf16[8,2,2048]{2,1,0:T(2,128)(2,1)S(1)}, u32[]{:S(2)}, u32[]{:S(2)}) %all-to-all-start) | async-done | bytes 65568 | tf_op jit(solution)/shard_map/all_to_all | solution.py:103
  16.0 1.1 %collective-permute-start = (bf16[64,1,256]{2,0,1:T(8,128)(2,1)S(1)}, bf16[64,1,256]{2,0,1:T(8,128)(2,1)S(1)}, u32[]{:S(2)}, u32[]{:S(2)}) collective-permute-start(bf16[64,1,256]{2,0,1:T(8,128)(2,1)S(1)} %maximum_convert_fusion), channel_id=1, source_target_pairs={{4,0},{8,4},{12,8},{16,12},{20,16},{24,20},{28,24},{0,28},{5,1},{9... | collective-permute-start | bytes 98312 | tf_op jit(solution)/shard_map/ppermute | solution.py:14
  17.2 1.3 %collective-permute-done.1 = bf16[64,1,256]{2,0,1:T(8,128)(2,1)S(1)} collective-permute-done((bf16[64,1,256]{2,0,1:T(8,128)(2,1)S(1)}, bf16[64,1,256]{2,0,1:T(8,128)(2,1)S(1)}, u32[]{:S(2)}, u32[]{:S(2)}) %collective-permute-start.1) | collective-permute-done | bytes 32800 | tf_op jit(solution)/shard_map/ppermute | solution.py:14
  18.8 5.5 %collective-permute-start.2 = (bf16[2,64,1,256]{3,1,2,0:T(8,128)(2,1)S(1)}, bf16[2,64,1,256]{3,1,2,0:T(8,128)(2,1)S(1)}, u32[]{:S(2)}, u32[]{:S(2)}) collective-permute-start(bf16[2,64,1,256]{3,1,2,0:T(8,128)(2,1)S(1)} %pad_maximum_fusion.2), channel_id=1, source_target_pairs={{1,0},{2,1},{3,2},{5,4},{6,5},{7,6},{9,8},{10,9},{11,10},{13,12},{... | collective-permute-start | bytes 196616 | tf_op jit(solution)/shard_map/ppermute | solution.py:20
  24.6 0.8 %copy.42 = bf16[16,2,128,1]{0,1,3,2:T(2,128)(2,1)} copy(bf16[16,2,128,1]{2,1,0,3:T(2,128)(2,1)S(1)} %bitcast.86) | data formatting | bytes 16384 | tf_op jit(solution)/shard_map/slice | solution.py:89
  25.3 0.7 %copy.43 = bf16[16,2,128,1]{0,1,3,2:T(2,128)(2,1)} copy(bf16[16,2,128,1]{2,1,0,3:T(2,128)(2,1)S(1)} %bitcast.85) | data formatting | bytes 16384 | tf_op jit(solution)/shard_map/slice | solution.py:89
  26.2 0.8 %copy.41 = bf16[16,2,128,1]{0,1,3,2:T(2,128)(2,1)} copy(bf16[16,2,128,1]{2,1,0,3:T(2,128)(2,1)S(1)} %bitcast.83) | data formatting | bytes 16384 | tf_op jit(solution)/shard_map/slice | solution.py:89
  28.0 0.9 %convert_bitcast_fusion = bf16[16,144,2,128]{1,0,2,3:T(8,128)(2,1)S(1)} fusion(bf16[16,2,128,1]{0,1,3,2:T(2,128)(2,1)S(1)} %copy.44, bf16[192,2,2,128]{0,1,2,3:T(2,128)(2,1)S(1)} %pad_maximum_fusion), kind=kOutput, calls=%fused_computation.1 | convolution fusion | flops 2949120 | bytes 1384448 | tf_op jit(solution)/shard_map/cxf,dxof->cdof/dot_general | solution.py:91
  28.9 2.5 %copy.39 = bf16[16,144,2,128]{3,2,1,0:T(2,128)(2,1)S(1)} copy(bf16[16,144,2,128]{1,0,2,3:T(8,128)(2,1)S(1)} %convert_bitcast_fusion) | data formatting | bytes 2359296 | tf_op jit(solution)/shard_map/cxf,dxof->cdof/transpose | solution.py:91
  32.1 1.1 %slice.124 = bf16[16,128,256]{2,1,0:T(8,128)(2,1)} slice(bf16[16,145,256]{2,1,0:T(8,128)(2,1)S(1)} %reshape.131), slice={[0:16], [0:128], [0:256]} | slice | bytes 2097152 | tf_op jit(solution)/shard_map/slice | solution.py:96
  33.2 0.9 %convert_bitcast_fusion.1 = bf16[16,144,2,128]{1,0,2,3:T(8,128)(2,1)S(1)} fusion(bf16[16,2,128,1]{0,1,3,2:T(2,128)(2,1)S(1)} %copy-done.5, bf16[192,2,2,128]{0,1,2,3:T(2,128)(2,1)S(1)} %pad_maximum_fusion), kind=kOutput, calls=%fused_computation.2 | convolution fusion | flops 2949120 | bytes 1384448 | tf_op jit(solution)/shard_map/cxf,dxof->cdof/dot_general | solution.py:91
  34.1 2.5 %copy.37 = bf16[16,144,2,128]{3,2,1,0:T(2,128)(2,1)S(1)} copy(bf16[16,144,2,128]{1,0,2,3:T(8,128)(2,1)S(1)} %convert_bitcast_fusion.1) | data formatting | bytes 2359296 | tf_op jit(solution)/shard_map/cxf,dxof->cdof/transpose | solution.py:91
  37.2 1.1 %slice.121 = bf16[16,128,256]{2,1,0:T(8,128)(2,1)} slice(bf16[16,145,256]{2,1,0:T(8,128)(2,1)S(1)} %reshape.129), slice={[0:16], [0:128], [0:256]} | slice | bytes 2097152 | tf_op jit(solution)/shard_map/slice | solution.py:96
  38.3 0.9 %convert_bitcast_fusion.2 = bf16[16,144,2,128]{1,0,2,3:T(8,128)(2,1)S(1)} fusion(bf16[16,2,128,1]{0,1,3,2:T(2,128)(2,1)S(1)} %copy-done.4, bf16[192,2,2,128]{0,1,2,3:T(2,128)(2,1)S(1)} %pad_maximum_fusion), kind=kOutput, calls=%fused_computation.3 | convolution fusion | flops 2949120 | bytes 1384448 | tf_op jit(solution)/shard_map/cxf,dxof->cdof/dot_general | solution.py:91
  39.2 2.5 %copy.35 = bf16[16,144,2,128]{3,2,1,0:T(2,128)(2,1)S(1)} copy(bf16[16,144,2,128]{1,0,2,3:T(8,128)(2,1)S(1)} %convert_bitcast_fusion.2) | data formatting | bytes 2359296 | tf_op jit(solution)/shard_map/cxf,dxof->cdof/transpose | solution.py:91
  42.3 1.1 %slice.118 = bf16[16,128,256]{2,1,0:T(8,128)(2,1)} slice(bf16[16,145,256]{2,1,0:T(8,128)(2,1)S(1)} %reshape.127), slice={[0:16], [0:128], [0:256]} | slice | bytes 2097152 | tf_op jit(solution)/shard_map/slice | solution.py:96
  43.5 0.8 %convert_bitcast_fusion.3 = bf16[16,144,2,128]{1,0,2,3:T(8,128)(2,1)S(1)} fusion(bf16[16,2,128,1]{0,1,3,2:T(2,128)(2,1)S(1)} %copy-done.3, bf16[192,2,2,128]{0,1,2,3:T(2,128)(2,1)S(1)} %pad_maximum_fusion), kind=kOutput, calls=%fused_computation.4 | convolution fusion | flops 2949120 | bytes 1384448 | tf_op jit(solution)/shard_map/cxf,dxof->cdof/dot_general | solution.py:91
  44.2 2.5 %copy.33 = bf16[16,144,2,128]{3,2,1,0:T(2,128)(2,1)S(1)} copy(bf16[16,144,2,128]{1,0,2,3:T(8,128)(2,1)S(1)} %convert_bitcast_fusion.3) | data formatting | bytes 2359296 | tf_op jit(solution)/shard_map/cxf,dxof->cdof/transpose | solution.py:91
  47.5 0.7 %copy-done = bf16[16,128,256]{2,1,0:T(8,128)(2,1)S(1)} copy-done((bf16[16,128,256]{2,1,0:T(8,128)(2,1)S(1)}, bf16[16,128,256]{2,1,0:T(8,128)(2,1)}, u32[]{:S(2)}) %copy-start) | copy-done | bytes 1048600
  49.0 2.3 %maximum_bitcast_fusion = bf16[1,64,128,256]{3,2,1,0:T(8,128)(2,1)} fusion(bf16[16,128,256]{2,1,0:T(8,128)(2,1)S(1)} %copy-done, bf16[16,128,256]{2,1,0:T(8,128)(2,1)S(1)} %copy-done.1, bf16[16,128,256]{2,1,0:T(8,128)(2,1)S(1)} %copy-done.2, bf16[16,128,256]{2,1,0:T(8,128)(2,1)S(1)} %slice.115), kind=kLoop, calls=%fused_computation | loop fusion | flops 6291456 | bytes 8388608 | tf_op jit(solution)/shard_map/broadcast_in_dim | solution.py:124
  (74 shorter events, 8.3 us)
Async XLA Ops:
  1.8 12.1 %all-to-all-start = ((bf16[8,2,2048]{2,1,0:T(2,128)(2,1)}), bf16[8,2,2048]{2,1,0:T(2,128)(2,1)S(1)}, u32[]{:S(2)}, u32[]{:S(2)}) async-start(bf16[8,2,2048]{2,1,0:T(2,128)(2,1)} %reshape.138), calls=%async_computation | async-start | bytes 131072 | tf_op jit(solution)/shard_map/all_to_all | solution.py:103
  15.6 2.8 %collective-permute-start.1 = (bf16[64,1,256]{2,0,1:T(8,128)(2,1)S(1)}, bf16[64,1,256]{2,0,1:T(8,128)(2,1)S(1)}, u32[]{:S(2)}, u32[]{:S(2)}) collective-permute-start(bf16[64,1,256]{2,0,1:T(8,128)(2,1)S(1)} %maximum_convert_fusion), channel_id=1, source_target_pairs={{8,0},{12,4},{16,8},{20,12},{24,16},{28,20},{0,24},{4,28},{9,1},{1... | collective-permute-start | bytes 98312 | tf_op jit(solution)/shard_map/ppermute | solution.py:14
  16.0 2.8 %collective-permute-start = (bf16[64,1,256]{2,0,1:T(8,128)(2,1)S(1)}, bf16[64,1,256]{2,0,1:T(8,128)(2,1)S(1)}, u32[]{:S(2)}, u32[]{:S(2)}) collective-permute-start(bf16[64,1,256]{2,0,1:T(8,128)(2,1)S(1)} %maximum_convert_fusion), channel_id=1, source_target_pairs={{4,0},{8,4},{12,8},{16,12},{20,16},{24,20},{28,24},{0,28},{5,1},{9... | collective-permute-start | bytes 98312 | tf_op jit(solution)/shard_map/ppermute | solution.py:14
  18.8 8.4 %collective-permute-start.2 = (bf16[2,64,1,256]{3,1,2,0:T(8,128)(2,1)S(1)}, bf16[2,64,1,256]{3,1,2,0:T(8,128)(2,1)S(1)}, u32[]{:S(2)}, u32[]{:S(2)}) collective-permute-start(bf16[2,64,1,256]{3,1,2,0:T(8,128)(2,1)S(1)} %pad_maximum_fusion.2), channel_id=1, source_target_pairs={{1,0},{2,1},{3,2},{5,4},{6,5},{7,6},{9,8},{10,9},{11,10},{13,12},{... | collective-permute-start | bytes 196616 | tf_op jit(solution)/shard_map/ppermute | solution.py:20
  32.1 1.1 %copy-start.5 = (bf16[16,2,128,1]{0,1,3,2:T(2,128)(2,1)S(1)}, bf16[16,2,128,1]{0,1,3,2:T(2,128)(2,1)}, u32[]{:S(2)}) copy-start(bf16[16,2,128,1]{0,1,3,2:T(2,128)(2,1)} %copy.43) | copy-start | bytes 24580
  37.2 1.1 %copy-start.4 = (bf16[16,2,128,1]{0,1,3,2:T(2,128)(2,1)S(1)}, bf16[16,2,128,1]{0,1,3,2:T(2,128)(2,1)}, u32[]{:S(2)}) copy-start(bf16[16,2,128,1]{0,1,3,2:T(2,128)(2,1)} %copy.42) | copy-start | bytes 24580
  41.9 1.6 %copy-start.3 = (bf16[16,2,128,1]{0,1,3,2:T(2,128)(2,1)S(1)}, bf16[16,2,128,1]{0,1,3,2:T(2,128)(2,1)}, u32[]{:S(2)}) copy-start(bf16[16,2,128,1]{0,1,3,2:T(2,128)(2,1)} %copy.41) | copy-start | bytes 24580
  46.9 1.2 %copy-start = (bf16[16,128,256]{2,1,0:T(8,128)(2,1)S(1)}, bf16[16,128,256]{2,1,0:T(8,128)(2,1)}, u32[]{:S(2)}) copy-start(bf16[16,128,256]{2,1,0:T(8,128)(2,1)} %slice.124) | copy-start | bytes 3145732
  47.4 1.3 %copy-start.1 = (bf16[16,128,256]{2,1,0:T(8,128)(2,1)S(1)}, bf16[16,128,256]{2,1,0:T(8,128)(2,1)}, u32[]{:S(2)}) copy-start(bf16[16,128,256]{2,1,0:T(8,128)(2,1)} %slice.121) | copy-start | bytes 3145732
  47.4 1.6 %copy-start.2 = (bf16[16,128,256]{2,1,0:T(8,128)(2,1)S(1)}, bf16[16,128,256]{2,1,0:T(8,128)(2,1)}, u32[]{:S(2)}) copy-start(bf16[16,128,256]{2,1,0:T(8,128)(2,1)} %slice.118) | copy-start | bytes 3145732
where the time goes:
time: 51.6 us; the launch traced here: 51.3 us
  local copies, waits for them, and re-layouts  23.8 us (46%)
  starting transfers between devices  13.5 us (26%)
  waiting for transfers between devices  5.81 us (11%)
  matrix products  4.04 us (8%)
  other arithmetic  3.7 us (7%)
    transpose x4, local copies, waits for them, and re-layouts, cross_block(): jnp.einsum('cxf,dxof->cdof', own_part, far_part, preferred_element_type=j...  9.84 us
    all_to_all x1, starting transfers between devices, body(): lax.all_to_all(strain, 'ta', split_axis=0, concat_axis=1, tiled=True)  6.38 us
    ppermute x1, starting transfers between devices, from_behind(): return lax.ppermute(block, axis, route)  5.55 us
    unnamed x21, local copies, waits for them, and re-layouts  4.04 us
    all_to_all x1, waiting for transfers between devices, body(): lax.all_to_all(strain, 'ta', split_axis=0, concat_axis=1, tiled=True)  3.94 us
    dot_general x4, matrix products, cross_block(): jnp.einsum('cxf,dxof->cdof', own_part, far_part, preferred_element_type=j...  3.4 us
    slice x4, local copies, waits for them, and re-layouts, cross_block(): banded = combined.reshape(step_rows, reach + 1, NFFT)[:, :LAGS]  3.38 us
    slice x9, local copies, waits for them, and re-layouts, cross_block(): own_part = own_pairs[first:first + step_rows]  2.43 us
  transfers between devices with their start and end apart: 4, of which 4 were waited for; matrix products, arithmetic and copies ran while one was open for 8% of the time, Pallas kernels for 0%

commit v1 on v0

--- a/solution.py
+++ b/solution.py
@@ -6,6 +6,12 @@
 NFFT = 256
 NF = 128
 LAGS = 128
+
+
+def stacked_exchange(x, mesh_axis, split, join):
+    pieces = jnp.split(x, lax.axis_size(mesh_axis), axis=split)
+    received = lax.all_to_all(jnp.stack(pieces), mesh_axis, 0, 0)
+    return jnp.concatenate(received, axis=join)
 
 
 def shifted(block, axis, distance):
@@ -100,7 +106,7 @@
 
 def body(strain, filter_taps):
     tap_count = filter_taps.shape[0]
-    regrouped = lax.all_to_all(strain, "ta", split_axis=0, concat_axis=1, tiled=True)
+    regrouped = stacked_exchange(strain, "ta", 0, 1)
     filtered = decimate(
         jnp.zeros((regrouped.shape[0], tap_count), jnp.float32),
         regrouped.astype(jnp.float32),

time: 51.6 us -> 56.9 us (1.10)
  local copies, waits for them, and re-layouts: 23.8 us -> 28.8 us
    unnamed x21 -> x27, local copies, waits for them, and re-layouts: 4.04 us -> 8.37 us
    another operation x0 -> x1, local copies, waits for them, and re-layouts: none -> 0.8 us  [stacked_exchange(): received = lax.all_to_all(jnp.stack(pieces), mesh_axis, 0, 0)]
where the time goes in v1:
time: 56.9 us; the launch traced here: 56.2 us
  local copies, waits for them, and re-layouts  28.8 us (51%)
  starting transfers between devices  13.5 us (24%)
  waiting for transfers between devices  5.81 us (10%)
  matrix products  4.04 us (7%)
  other arithmetic  3.7 us (7%)
    transpose x4, local copies, waits for them, and re-layouts, cross_block(): jnp.einsum('cxf,dxof->cdof', own_part, far_part, preferred_element_type=j...  9.84 us
    unnamed x27, local copies, waits for them, and re-layouts  8.37 us
    all_to_all x1, starting transfers between devices, stacked_exchange(): received = lax.all_to_all(jnp.stack(pieces), mesh_axis, 0, 0)  6.38 us
    ppermute x1, starting transfers between devices, from_behind(): return lax.ppermute(block, axis, route)  5.55 us
    all_to_all x1, waiting for transfers between devices, stacked_exchange(): received = lax.all_to_all(jnp.stack(pieces), mesh_axis, 0, 0)  3.94 us
    dot_general x4, matrix products, cross_block(): jnp.einsum('cxf,dxof->cdof', own_part, far_part, preferred_element_type=j...  3.4 us
    slice x4, local copies, waits for them, and re-layouts, cross_block(): banded = combined.reshape(step_rows, reach + 1, NFFT)[:, :LAGS]  3.38 us
    slice x9, local copies, waits for them, and re-layouts, cross_block(): own_part = own_pairs[first:first + step_rows]  2.43 us
  transfers between devices with their start and end apart: 4, of which 4 were waited for; matrix products, arithmetic and copies ran while one was open for 8% of the time, Pallas kernels for 0%

profile of v1, /device:TPU:1, one launch (start us, length us, event | category | flops | bytes accessed | tf_op | source)
XLA Modules:
  0.0 56.2 jit_solution(14212993251908456417)
XLA Ops:
  0.7 0.8 %constant_dynamic-update-slice_fusion.6 = bf16[8,64,64]{1,2,0:T(8,128)(2,1)S(1)} fusion(bf16[8,64,64]{1,2,0:T(8,128)(2,1)S(1)} %constant_dynamic-update-slice_fusion.7, bf16[512,64]{0,1:T(8,128)(2,1)} %param.2), kind=kLoop, calls=%fused_computation.57 | loop fusion | bytes 24576
  2.2 0.8 %constant_dynamic-update-slice_fusion.4 = bf16[8,64,64]{1,2,0:T(8,128)(2,1)S(1)} fusion(bf16[8,64,64]{1,2,0:T(8,128)(2,1)S(1)} %constant_dynamic-update-slice_fusion.5, bf16[512,64]{0,1:T(8,128)(2,1)} %param.2), kind=kLoop, calls=%fused_computation.55 | loop fusion | bytes 24576
  3.8 0.8 %constant_dynamic-update-slice_fusion.2 = bf16[8,64,64]{1,2,0:T(8,128)(2,1)S(1)} fusion(bf16[8,64,64]{1,2,0:T(8,128)(2,1)S(1)} %constant_dynamic-update-slice_fusion.3, bf16[512,64]{0,1:T(8,128)(2,1)} %param.2), kind=kLoop, calls=%fused_computation.53 | loop fusion | bytes 24576
  5.3 0.8 %constant_dynamic-update-slice_fusion = bf16[8,64,64]{1,2,0:T(8,128)(2,1)S(1)} fusion(bf16[8,64,64]{1,2,0:T(8,128)(2,1)S(1)} %constant_dynamic-update-slice_fusion.1, bf16[512,64]{0,1:T(8,128)(2,1)} %param.2), kind=kLoop, calls=%fused_computation.51 | loop fusion | bytes 24576 | tf_op jit(solution)/shard_map/stack | solution.py:13
  6.1 0.8 %reshape.137 = bf16[8,2,2048]{2,1,0:T(2,128)(2,1)} reshape(bf16[8,64,64]{2,1,0:T(8,128)(2,1)S(1)} %bitcast.98) | data formatting | bytes 131072
  6.9 6.4 %all-to-all-start = ((bf16[8,2,2048]{2,1,0:T(2,128)(2,1)}), bf16[8,2,2048]{2,1,0:T(2,128)(2,1)S(1)}, u32[]{:S(2)}, u32[]{:S(2)}) async-start(bf16[8,2,2048]{2,1,0:T(2,128)(2,1)} %reshape.137), calls=%async_computation | async-start | bytes 131072 | tf_op jit(solution)/shard_map/all_to_all | solution.py:13
  15.1 3.9 %all-to-all-done = bf16[8,2,2048]{2,1,0:T(2,128)(2,1)S(1)} async-done(((bf16[8,2,2048]{2,1,0:T(2,128)(2,1)}), bf16[8,2,2048]{2,1,0:T(2,128)(2,1)S(1)}, u32[]{:S(2)}, u32[]{:S(2)}) %all-to-all-start) | async-done | bytes 65568 | tf_op jit(solution)/shard_map/all_to_all | solution.py:13
  21.0 1.1 %collective-permute-start = (bf16[64,1,256]{2,0,1:T(8,128)(2,1)S(1)}, bf16[64,1,256]{2,0,1:T(8,128)(2,1)S(1)}, u32[]{:S(2)}, u32[]{:S(2)}) collective-permute-start(bf16[64,1,256]{2,0,1:T(8,128)(2,1)S(1)} %maximum_convert_fusion), channel_id=1, source_target_pairs={{4,0},{8,4},{12,8},{16,12},{20,16},{24,20},{28,24},{0,28},{5,1},{9... | collective-permute-start | bytes 98312 | tf_op jit(solution)/shard_map/ppermute | solution.py:20
  22.1 1.3 %collective-permute-done.1 = bf16[64,1,256]{2,0,1:T(8,128)(2,1)S(1)} collective-permute-done((bf16[64,1,256]{2,0,1:T(8,128)(2,1)S(1)}, bf16[64,1,256]{2,0,1:T(8,128)(2,1)S(1)}, u32[]{:S(2)}, u32[]{:S(2)}) %collective-permute-start.1) | collective-permute-done | bytes 32800 | tf_op jit(solution)/shard_map/ppermute | solution.py:20
  23.8 5.5 %collective-permute-start.2 = (bf16[2,64,1,256]{3,1,2,0:T(8,128)(2,1)S(1)}, bf16[2,64,1,256]{3,1,2,0:T(8,128)(2,1)S(1)}, u32[]{:S(2)}, u32[]{:S(2)}) collective-permute-start(bf16[2,64,1,256]{3,1,2,0:T(8,128)(2,1)S(1)} %pad_maximum_fusion.2), channel_id=1, source_target_pairs={{1,0},{2,1},{3,2},{5,4},{6,5},{7,6},{9,8},{10,9},{11,10},{13,12},{... | collective-permute-start | bytes 196616 | tf_op jit(solution)/shard_map/ppermute | solution.py:26
  29.5 0.8 %copy.26 = bf16[16,2,128,1]{0,1,3,2:T(2,128)(2,1)} copy(bf16[16,2,128,1]{2,1,0,3:T(2,128)(2,1)S(1)} %bitcast.106) | data formatting | bytes 16384 | tf_op jit(solution)/shard_map/slice | solution.py:95
  31.2 0.8 %copy.25 = bf16[16,2,128,1]{0,1,3,2:T(2,128)(2,1)} copy(bf16[16,2,128,1]{2,1,0,3:T(2,128)(2,1)S(1)} %bitcast.103) | data formatting | bytes 16384 | tf_op jit(solution)/shard_map/slice | solution.py:95
  33.0 0.9 %convert_bitcast_fusion = bf16[16,144,2,128]{1,0,2,3:T(8,128)(2,1)S(1)} fusion(bf16[16,2,128,1]{0,1,3,2:T(2,128)(2,1)S(1)} %copy.28, bf16[192,2,2,128]{0,1,2,3:T(2,128)(2,1)S(1)} %pad_maximum_fusion), kind=kOutput, calls=%fused_computation.1 | convolution fusion | flops 2949120 | bytes 1384448 | tf_op jit(solution)/shard_map/cxf,dxof->cdof/dot_general | solution.py:97
  33.9 2.5 %copy.23 = bf16[16,144,2,128]{3,2,1,0:T(2,128)(2,1)S(1)} copy(bf16[16,144,2,128]{1,0,2,3:T(8,128)(2,1)S(1)} %convert_bitcast_fusion) | data formatting | bytes 2359296 | tf_op jit(solution)/shard_map/cxf,dxof->cdof/transpose | solution.py:97
  37.1 1.1 %slice.124 = bf16[16,128,256]{2,1,0:T(8,128)(2,1)} slice(bf16[16,145,256]{2,1,0:T(8,128)(2,1)S(1)} %reshape.130), slice={[0:16], [0:128], [0:256]} | slice | bytes 2097152 | tf_op jit(solution)/shard_map/slice | solution.py:102
  38.1 0.9 %convert_bitcast_fusion.1 = bf16[16,144,2,128]{1,0,2,3:T(8,128)(2,1)S(1)} fusion(bf16[16,2,128,1]{0,1,3,2:T(2,128)(2,1)S(1)} %copy-done.5, bf16[192,2,2,128]{0,1,2,3:T(2,128)(2,1)S(1)} %pad_maximum_fusion), kind=kOutput, calls=%fused_computation.2 | convolution fusion | flops 2949120 | bytes 1384448 | tf_op jit(solution)/shard_map/cxf,dxof->cdof/dot_general | solution.py:97
  39.0 2.5 %copy.21 = bf16[16,144,2,128]{3,2,1,0:T(2,128)(2,1)S(1)} copy(bf16[16,144,2,128]{1,0,2,3:T(8,128)(2,1)S(1)} %convert_bitcast_fusion.1) | data formatting | bytes 2359296 | tf_op jit(solution)/shard_map/cxf,dxof->cdof/transpose | solution.py:97
  42.2 1.1 %slice.121 = bf16[16,128,256]{2,1,0:T(8,128)(2,1)} slice(bf16[16,145,256]{2,1,0:T(8,128)(2,1)S(1)} %reshape.128), slice={[0:16], [0:128], [0:256]} | slice | bytes 2097152 | tf_op jit(solution)/shard_map/slice | solution.py:102
  43.3 0.9 %convert_bitcast_fusion.2 = bf16[16,144,2,128]{1,0,2,3:T(8,128)(2,1)S(1)} fusion(bf16[16,2,128,1]{0,1,3,2:T(2,128)(2,1)S(1)} %copy-done.4, bf16[192,2,2,128]{0,1,2,3:T(2,128)(2,1)S(1)} %pad_maximum_fusion), kind=kOutput, calls=%fused_computation.3 | convolution fusion | flops 2949120 | bytes 1384448 | tf_op jit(solution)/shard_map/cxf,dxof->cdof/dot_general | solution.py:97
  44.2 2.5 %copy.19 = bf16[16,144,2,128]{3,2,1,0:T(2,128)(2,1)S(1)} copy(bf16[16,144,2,128]{1,0,2,3:T(8,128)(2,1)S(1)} %convert_bitcast_fusion.2) | data formatting | bytes 2359296 | tf_op jit(solution)/shard_map/cxf,dxof->cdof/transpose | solution.py:97
  47.3 1.1 %slice.118 = bf16[16,128,256]{2,1,0:T(8,128)(2,1)} slice(bf16[16,145,256]{2,1,0:T(8,128)(2,1)S(1)} %reshape.126), slice={[0:16], [0:128], [0:256]} | slice | bytes 2097152 | tf_op jit(solution)/shard_map/slice | solution.py:102
  48.4 0.8 %convert_bitcast_fusion.3 = bf16[16,144,2,128]{1,0,2,3:T(8,128)(2,1)S(1)} fusion(bf16[16,2,128,1]{0,1,3,2:T(2,128)(2,1)S(1)} %copy-done.3, bf16[192,2,2,128]{0,1,2,3:T(2,128)(2,1)S(1)} %pad_maximum_fusion), kind=kOutput, calls=%fused_computation.4 | convolution fusion | flops 2949120 | bytes 1384448 | tf_op jit(solution)/shard_map/cxf,dxof->cdof/dot_general | solution.py:97
  49.2 2.5 %copy.17 = bf16[16,144,2,128]{3,2,1,0:T(2,128)(2,1)S(1)} copy(bf16[16,144,2,128]{1,0,2,3:T(8,128)(2,1)S(1)} %convert_bitcast_fusion.3) | data formatting | bytes 2359296 | tf_op jit(solution)/shard_map/cxf,dxof->cdof/transpose | solution.py:97
  54.0 2.3 %maximum_bitcast_fusion = bf16[1,64,128,256]{3,2,1,0:T(8,128)(2,1)} fusion(bf16[16,128,256]{2,1,0:T(8,128)(2,1)S(1)} %copy-done, bf16[16,128,256]{2,1,0:T(8,128)(2,1)S(1)} %copy-done.1, bf16[16,128,256]{2,1,0:T(8,128)(2,1)S(1)} %copy-done.2, bf16[16,128,256]{2,1,0:T(8,128)(2,1)S(1)} %slice.115), kind=kLoop, calls=%fused_computation | loop fusion | flops 6291456 | bytes 8388608 | tf_op jit(solution)/shard_map/broadcast_in_dim | solution.py:130
  (80 shorter events, 13.2 us)
Async XLA Ops:
  6.9 12.1 %all-to-all-start = ((bf16[8,2,2048]{2,1,0:T(2,128)(2,1)}), bf16[8,2,2048]{2,1,0:T(2,128)(2,1)S(1)}, u32[]{:S(2)}, u32[]{:S(2)}) async-start(bf16[8,2,2048]{2,1,0:T(2,128)(2,1)} %reshape.137), calls=%async_computation | async-start | bytes 131072 | tf_op jit(solution)/shard_map/all_to_all | solution.py:13
  20.6 2.8 %collective-permute-start.1 = (bf16[64,1,256]{2,0,1:T(8,128)(2,1)S(1)}, bf16[64,1,256]{2,0,1:T(8,128)(2,1)S(1)}, u32[]{:S(2)}, u32[]{:S(2)}) collective-permute-start(bf16[64,1,256]{2,0,1:T(8,128)(2,1)S(1)} %maximum_convert_fusion), channel_id=1, source_target_pairs={{8,0},{12,4},{16,8},{20,12},{24,16},{28,20},{0,24},{4,28},{9,1},{1... | collective-permute-start | bytes 98312 | tf_op jit(solution)/shard_map/ppermute | solution.py:20
  21.0 2.8 %collective-permute-start = (bf16[64,1,256]{2,0,1:T(8,128)(2,1)S(1)}, bf16[64,1,256]{2,0,1:T(8,128)(2,1)S(1)}, u32[]{:S(2)}, u32[]{:S(2)}) collective-permute-start(bf16[64,1,256]{2,0,1:T(8,128)(2,1)S(1)} %maximum_convert_fusion), channel_id=1, source_target_pairs={{4,0},{8,4},{12,8},{16,12},{20,16},{24,20},{28,24},{0,28},{5,1},{9... | collective-permute-start | bytes 98312 | tf_op jit(solution)/shard_map/ppermute | solution.py:20
  23.8 8.4 %collective-permute-start.2 = (bf16[2,64,1,256]{3,1,2,0:T(8,128)(2,1)S(1)}, bf16[2,64,1,256]{3,1,2,0:T(8,128)(2,1)S(1)}, u32[]{:S(2)}, u32[]{:S(2)}) collective-permute-start(bf16[2,64,1,256]{3,1,2,0:T(8,128)(2,1)S(1)} %pad_maximum_fusion.2), channel_id=1, source_target_pairs={{1,0},{2,1},{3,2},{5,4},{6,5},{7,6},{9,8},{10,9},{11,10},{13,12},{... | collective-permute-start | bytes 196616 | tf_op jit(solution)/shard_map/ppermute | solution.py:26
  37.0 1.1 %copy-start.5 = (bf16[16,2,128,1]{0,1,3,2:T(2,128)(2,1)S(1)}, bf16[16,2,128,1]{0,1,3,2:T(2,128)(2,1)}, u32[]{:S(2)}) copy-start(bf16[16,2,128,1]{0,1,3,2:T(2,128)(2,1)} %copy.27) | copy-start | bytes 24580
  42.2 1.1 %copy-start.4 = (bf16[16,2,128,1]{0,1,3,2:T(2,128)(2,1)S(1)}, bf16[16,2,128,1]{0,1,3,2:T(2,128)(2,1)}, u32[]{:S(2)}) copy-start(bf16[16,2,128,1]{0,1,3,2:T(2,128)(2,1)} %copy.26) | copy-start | bytes 24580
  46.9 1.6 %copy-start.3 = (bf16[16,2,128,1]{0,1,3,2:T(2,128)(2,1)S(1)}, bf16[16,2,128,1]{0,1,3,2:T(2,128)(2,1)}, u32[]{:S(2)}) copy-start(bf16[16,2,128,1]{0,1,3,2:T(2,128)(2,1)} %copy.25) | copy-start | bytes 24580
  51.9 1.2 %copy-start = (bf16[16,128,256]{2,1,0:T(8,128)(2,1)S(1)}, bf16[16,128,256]{2,1,0:T(8,128)(2,1)}, u32[]{:S(2)}) copy-start(bf16[16,128,256]{2,1,0:T(8,128)(2,1)} %slice.124) | copy-start | bytes 3145732
  52.4 1.3 %copy-start.1 = (bf16[16,128,256]{2,1,0:T(8,128)(2,1)S(1)}, bf16[16,128,256]{2,1,0:T(8,128)(2,1)}, u32[]{:S(2)}) copy-start(bf16[16,128,256]{2,1,0:T(8,128)(2,1)} %slice.121) | copy-start | bytes 3145732
  52.4 1.6 %copy-start.2 = (bf16[16,128,256]{2,1,0:T(8,128)(2,1)S(1)}, bf16[16,128,256]{2,1,0:T(8,128)(2,1)}, u32[]{:S(2)}) copy-start(bf16[16,128,256]{2,1,0:T(8,128)(2,1)} %slice.118) | copy-start | bytes 3145732
